TPU v7x, 32 devices: a whole 2x2x4 slice. The times are simulated.
32 devices in a mesh: shard: 2 (over core), context: 4 (over z), tensor: 4 (over y, x).
Axes of the slice: x: 2, y: 2, z: 4, core: 2. Of those that a mesh axis runs over, the one named last changes fastest.
Arguments:
- inputs: bfloat16 [2, 2048, 2048], P('shard', 'context'), may hold values from -6 to 6
- segments: int32 [2, 2048], P('shard', 'context'), may hold values from 0 to 2, as said below
- positions: int32 [2, 2048], P('shard', 'context'), may hold values from 0 to 2047, as said below
- w_q: bfloat16 [2048, 2048], P(('shard', 'context'), 'tensor'), may hold values from -0.125 to 0.125
- w_k: bfloat16 [2048, 2048], P(('shard', 'context'), 'tensor'), may hold values from -0.125 to 0.125
- w_v: bfloat16 [2048, 2048], P(('shard', 'context'), 'tensor'), may hold values from -0.125 to 0.125
- w_o: bfloat16 [2048, 2048], P(('shard', 'context'), 'tensor'), may hold values from -0.75 to 0.75
- w_gate: bfloat16 [2048, 8192], P(('shard', 'context'), 'tensor'), may hold values from -0.125 to 0.125
- w_up: bfloat16 [2048, 8192], P(('shard', 'context'), 'tensor'), may hold values from -0.125 to 0.125
- w_down: bfloat16 [2048, 8192], P(('shard', 'context'), 'tensor'), may hold values from -0.0625 to 0.0625
- g_attn: bfloat16 [2048], P(('shard', 'context')), may hold values from 0.5 to 1.5
- g_mlp: bfloat16 [2048], P(('shard', 'context')), may hold values from 0.5 to 1.5
- d_out: bfloat16 [2, 2048, 2048], P('shard', 'context'), may hold values from -6 to 6
Outputs:
- out: bfloat16 [2, 2048, 2048], P('shard', 'context')
- d_x: bfloat16 [2, 2048, 2048], P('shard', 'context')
- d_w_q: float32 [2048, 2048], P(('shard', 'context'), 'tensor')
- d_w_k: float32 [2048, 2048], P(('shard', 'context'), 'tensor')
- d_w_v: float32 [2048, 2048], P(('shard', 'context'), 'tensor')
- d_w_o: float32 [2048, 2048], P(('shard', 'context'), 'tensor')
- d_w_gate: float32 [2048, 8192], P(('shard', 'context'), 'tensor')
- d_w_up: float32 [2048, 8192], P(('shard', 'context'), 'tensor')
- d_w_down: float32 [2048, 8192], P(('shard', 'context'), 'tensor')
- d_g_attn: float32 [2048], P(('shard', 'context'))
- d_g_mlp: float32 [2048], P(('shard', 'context'))
Inputs may be any that keep to these rules, and one draw needn't show every extreme that they name: In each sequence the positions are a permutation of 0 to 2047, laid out by halves of 512 tokens: with p a permutation of the context indices, device c holds either halves 2 * p(c) and 2 * p(c) + 1 in order, or halves p(c) and 7 - p(c). `segments`: segment numbers never fall as the position grows; the first position of a sequence is in segment 0, and every sequence holds exactly 3 documents.
All inputs are finite; a program needn't handle non-finite values.
Results may differ from a plain program's by a relative error of at most 0.024.
Values may be sent and summed in bfloat16 or wider, within the bound.
No kernel may reach another device: no remote copies, remote signals or barrier semaphores. Data moves between devices by JAX's collectives and lax.ppermute only.
A program may use at most 192 MiB of HBM per device.

v0:
```python
import math
import jax
import jax.numpy as jnp
from jax import lax
from jax.sharding import PartitionSpec as P

HD = 64
EPS = 1e-05
THETA = 130000.0
NEG = -1e30


def passed_along(value, axis, steps):
    count = lax.axis_size(axis)
    pairs = [(source, (source + steps) % count) for source in range(count)]
    return lax.ppermute(value, axis, pairs)


def rope_tables(position):
    index = jnp.arange(HD // 2, dtype=jnp.float32)
    inverse = jnp.power(jnp.float32(THETA), -2.0 * index / HD)
    angle = position.astype(jnp.float32)[:, None] * inverse[None, :]
    return (jnp.cos(angle), jnp.sin(angle))


def rotate(tensor, cosine, sine):
    half = tensor.shape[-1] // 2
    first = tensor[..., :half]
    second = tensor[..., half:]
    cosine = cosine[:, None, :]
    sine = sine[:, None, :]
    return jnp.concatenate(
        [first * cosine - second * sine, second * cosine + first * sine], axis=-1
    )


def rotate_back(grad, cosine, sine):
    half = grad.shape[-1] // 2
    first = grad[..., :half]
    second = grad[..., half:]
    cosine = cosine[:, None, :]
    sine = sine[:, None, :]
    return jnp.concatenate(
        [first * cosine + second * sine, second * cosine - first * sine], axis=-1
    )


def normalize(value):
    inv_rms = lax.rsqrt(jnp.mean(value * value, axis=-1, keepdims=True) + EPS)
    return (value * inv_rms, inv_rms)


def norm_back(grad, normed, inv_rms, gain):
    scaled = grad * gain.astype(jnp.float32)
    return inv_rms * (scaled - normed * jnp.mean(scaled * normed, axis=-1, keepdims=True))


def contract_last(left, right):
    return lax.dot_general(
        left, right, (((1,), (1,)), ((), ())), preferred_element_type=jnp.float32
    )


def contract_first(left, right):
    return lax.dot_general(
        left, right, (((0,), (0,)), ((), ())), preferred_element_type=jnp.float32
    )


def branch_total(partial_sum):
    return lax.psum(partial_sum.astype(jnp.bfloat16), "tensor").astype(jnp.float32)


def input_total(partial_sum):
    return lax.psum(partial_sum.astype(jnp.bfloat16), "tensor").astype(jnp.float32)


def pass_grads(grad_key, grad_value):
    return (
        passed_along(grad_key.astype(jnp.bfloat16), "context", 1).astype(grad_key.dtype),
        passed_along(grad_value.astype(jnp.bfloat16), "context", 1).astype(grad_value.dtype),
    )


def key_scores(query_heads, query_seg, query_pos, piece):
    key_flat, value_flat, key_seg, key_pos = piece
    heads = query_heads.shape[1]
    key_heads = key_flat.reshape(key_flat.shape[0], heads, HD)
    value_heads = value_flat.reshape(value_flat.shape[0], heads, HD)
    scores = jnp.einsum(
        "qhd,khd->hqk", query_heads, key_heads, preferred_element_type=jnp.float32
    ) * (1.0 / math.sqrt(HD))
    allowed = (query_seg[:, None] == key_seg[None, :]) & (key_pos[None, :] <= query_pos[:, None])
    return (jnp.where(allowed[None], scores, NEG), allowed, key_heads, value_heads)


def forward_fold(stats, piece, query_heads, query_seg, query_pos):
    peak, total, accum = stats
    scores, allowed, key_heads, value_heads = key_scores(query_heads, query_seg, query_pos, piece)
    new_peak = jnp.maximum(peak, jnp.max(scores, axis=-1))
    weights = jnp.where(allowed[None], jnp.exp(scores - new_peak[..., None]), 0.0)
    factor = jnp.exp(peak - new_peak)
    total = total * factor + jnp.sum(weights, axis=-1)
    accum = accum * factor[..., None] + jnp.einsum(
        "hqk,khd->hqd",
        weights.astype(jnp.bfloat16),
        value_heads,
        preferred_element_type=jnp.float32,
    )
    return (new_peak, total, accum)


def backward_piece(piece, query_heads, grad_heads, log_total, inner, query_seg, query_pos):
    scores, allowed, key_heads, value_heads = key_scores(query_heads, query_seg, query_pos, piece)
    probs = jnp.where(allowed[None], jnp.exp(scores - log_total[..., None]), 0.0)
    grad_value = jnp.einsum(
        "hqk,qhd->khd", probs.astype(jnp.bfloat16), grad_heads, preferred_element_type=jnp.float32
    )
    grad_probs = jnp.einsum(
        "qhd,khd->hqk", grad_heads, value_heads, preferred_element_type=jnp.float32
    )
    grad_scores = (probs * (grad_probs - inner[..., None]) * (1.0 / math.sqrt(HD))).astype(
        jnp.bfloat16
    )
    grad_query = jnp.einsum(
        "hqk,khd->qhd", grad_scores, key_heads, preferred_element_type=jnp.float32
    )
    grad_key = jnp.einsum(
        "hqk,qhd->khd", grad_scores, query_heads, preferred_element_type=jnp.float32
    )
    key_rows = grad_key.shape[0]
    return (grad_query, grad_key.reshape(key_rows, -1), grad_value.reshape(key_rows, -1))


def on_device(
    inputs, segments, positions, w_q, w_k, w_v, w_o, w_gate, w_up, w_down, g_attn, g_mlp, d_out
):
    f32 = jnp.float32
    bf16 = jnp.bfloat16
    rows = inputs.shape[1]
    width = inputs.shape[2]
    tokens = inputs.reshape(rows, width)
    segment = segments.reshape(rows)
    position = positions.reshape(rows)
    fetched = (
        lax.all_gather(w_q, ("shard", "context"), axis=0, tiled=True),
        lax.all_gather(w_k, ("shard", "context"), axis=0, tiled=True),
        lax.all_gather(w_v, ("shard", "context"), axis=0, tiled=True),
        lax.all_gather(w_o, ("shard", "context"), axis=0, tiled=True),
        lax.all_gather(w_gate, ("shard", "context"), axis=0, tiled=True),
        lax.all_gather(w_up, ("shard", "context"), axis=0, tiled=True),
        lax.all_gather(w_down, ("shard", "context"), axis=0, tiled=True),
        lax.all_gather(g_attn, ("shard", "context"), axis=0, tiled=True),
        lax.all_gather(g_mlp, ("shard", "context"), axis=0, tiled=True),
    )
    full_q, full_k, full_v, full_o, full_gate, full_up, full_down, gain_attn, gain_mlp = fetched
    heads = full_q.shape[1] // HD
    cosine, sine = rope_tables(position)
    resid1 = tokens.astype(f32)
    norm1, inv1 = normalize(resid1)
    h1 = (norm1 * gain_attn.astype(f32)).astype(bf16)
    query = rotate(
        jnp.dot(h1, full_q, preferred_element_type=f32).reshape(rows, heads, HD), cosine, sine
    ).astype(bf16)
    key_flat = (
        rotate(
            jnp.dot(h1, full_k, preferred_element_type=f32).reshape(rows, heads, HD), cosine, sine
        )
        .astype(bf16)
        .reshape(rows, heads * HD)
    )
    value_flat = jnp.dot(h1, full_v, preferred_element_type=f32).astype(bf16)
    start_stats = (
        jnp.full((heads, rows), NEG, f32),
        jnp.zeros((heads, rows), f32),
        jnp.zeros((heads, rows, HD), f32),
    )
    stats = forward_fold(
        start_stats, (key_flat, value_flat, segment, position), query, segment, position
    )

    def cycle_turn(index, carry):
        moving_key, moving_value, moving_seg, moving_pos, current = carry
        moving_key, moving_value, moving_seg, moving_pos = passed_along(
            (moving_key, moving_value, moving_seg, moving_pos), "context", 1
        )
        current = forward_fold(
            current, (moving_key, moving_value, moving_seg, moving_pos), query, segment, position
        )
        return (moving_key, moving_value, moving_seg, moving_pos, current)

    stats = lax.fori_loop(
        0,
        lax.axis_size("context") - 1,
        cycle_turn,
        (key_flat, value_flat, segment, position, stats),
    )[4]
    peak, total, accum = stats
    attended = jnp.transpose(accum / total[..., None], (1, 0, 2)).astype(bf16)
    log_total = peak + jnp.log(total)
    attended_flat = attended.reshape(rows, heads * HD)
    attn_partial = contract_last(attended_flat, full_o)
    resid2 = resid1 + branch_total(attn_partial)
    norm2, inv2 = normalize(resid2)
    h2_part = (norm2 * gain_mlp.astype(f32)).astype(bf16)
    gate = jnp.dot(h2_part, full_gate, preferred_element_type=f32)
    up = jnp.dot(h2_part, full_up, preferred_element_type=f32)
    active = jax.nn.silu(gate)
    hidden = (active * up).astype(bf16)
    mlp_partial = contract_last(hidden, full_down)
    result = (resid2 + branch_total(mlp_partial)).astype(bf16)
    fetched = (
        lax.all_gather(w_q, ("shard", "context"), axis=0, tiled=True),
        lax.all_gather(w_k, ("shard", "context"), axis=0, tiled=True),
        lax.all_gather(w_v, ("shard", "context"), axis=0, tiled=True),
        lax.all_gather(w_o, ("shard", "context"), axis=0, tiled=True),
        lax.all_gather(w_gate, ("shard", "context"), axis=0, tiled=True),
        lax.all_gather(w_up, ("shard", "context"), axis=0, tiled=True),
        lax.all_gather(w_down, ("shard", "context"), axis=0, tiled=True),
        lax.all_gather(g_attn, ("shard", "context"), axis=0, tiled=True),
        lax.all_gather(g_mlp, ("shard", "context"), axis=0, tiled=True),
    )
    full_q, full_k, full_v, full_o, full_gate, full_up, full_down, gain_attn, gain_mlp = fetched
    grad_y = d_out.reshape(rows, width)
    grad_hidden = jnp.dot(grad_y, full_down, preferred_element_type=f32)
    sigma = jax.nn.sigmoid(gate)
    grad_gate = (grad_hidden * up * sigma * (1.0 + gate * (1.0 - sigma))).astype(bf16)
    grad_up = (grad_hidden * active).astype(bf16)
    h2_grad_partial = contract_last(grad_gate, full_gate) + contract_last(grad_up, full_up)
    grad_h2 = input_total(h2_grad_partial)
    grad_gmlp = jnp.sum(grad_h2 * norm2, axis=0)
    grad_resid = grad_y.astype(f32) + norm_back(grad_h2, norm2, inv2, gain_mlp)
    grad_resid_part = grad_resid.astype(bf16)
    grad_heads = (
        jnp.dot(grad_resid_part, full_o, preferred_element_type=f32)
        .astype(bf16)
        .reshape(rows, heads, HD)
    )
    inner = jnp.sum(grad_heads.astype(f32) * attended.astype(f32), axis=-1).T

    def piece_grads(piece):
        return backward_piece(piece, query, grad_heads, log_total, inner, segment, position)

    grad_query, grad_key, grad_value = piece_grads((key_flat, value_flat, segment, position))

    def grad_turn(index, carry):
        moving_key, moving_value, moving_seg, moving_pos, acc_query, acc_key, acc_value = carry
        moving_key, moving_value, moving_seg, moving_pos = passed_along(
            (moving_key, moving_value, moving_seg, moving_pos), "context", 1
        )
        acc_key, acc_value = pass_grads(acc_key, acc_value)
        part_query, part_key, part_value = piece_grads(
            (moving_key, moving_value, moving_seg, moving_pos)
        )
        return (
            moving_key,
            moving_value,
            moving_seg,
            moving_pos,
            acc_query + part_query,
            acc_key + part_key,
            acc_value + part_value,
        )

    carried = lax.fori_loop(
        0,
        lax.axis_size("context") - 1,
        grad_turn,
        (key_flat, value_flat, segment, position, grad_query, grad_key, grad_value),
    )
    grad_query = carried[4]
    grad_key, grad_value = pass_grads(carried[5], carried[6])
    grad_qin = rotate_back(grad_query, cosine, sine).astype(bf16).reshape(rows, heads * HD)
    grad_kin = (
        rotate_back(grad_key.reshape(rows, heads, HD), cosine, sine)
        .astype(bf16)
        .reshape(rows, heads * HD)
    )
    grad_vin = grad_value.astype(bf16)
    h1_grad_partial = (
        contract_last(grad_qin, full_q)
        + contract_last(grad_kin, full_k)
        + contract_last(grad_vin, full_v)
    )
    grad_h1 = input_total(h1_grad_partial)
    grad_gattn = jnp.sum(grad_h1 * norm1, axis=0)
    grad_x_part = (grad_resid + norm_back(grad_h1, norm1, inv1, gain_attn)).astype(bf16)
    grad_wq = contract_first(h1, grad_qin)
    grad_wk = contract_first(h1, grad_kin)
    grad_wv = contract_first(h1, grad_vin)
    grad_wo = contract_first(grad_resid_part, attended_flat)
    grad_wgate = contract_first(h2_part, grad_gate)
    grad_wup = contract_first(h2_part, grad_up)
    grad_wdown = contract_first(grad_y, hidden)
    reduced = (
        lax.psum_scatter(
            grad_wq.astype(jnp.bfloat16), ("shard", "context"), scatter_dimension=0, tiled=True
        ).astype(jnp.float32),
        lax.psum_scatter(
            grad_wk.astype(jnp.bfloat16), ("shard", "context"), scatter_dimension=0, tiled=True
        ).astype(jnp.float32),
        lax.psum_scatter(
            grad_wv.astype(jnp.bfloat16), ("shard", "context"), scatter_dimension=0, tiled=True
        ).astype(jnp.float32),
        lax.psum_scatter(
            grad_wo.astype(jnp.bfloat16), ("shard", "context"), scatter_dimension=0, tiled=True
        ).astype(jnp.float32),
        lax.psum_scatter(
            grad_wgate.astype(jnp.bfloat16), ("shard", "context"), scatter_dimension=0, tiled=True
        ).astype(jnp.float32),
        lax.psum_scatter(
            grad_wup.astype(jnp.bfloat16), ("shard", "context"), scatter_dimension=0, tiled=True
        ).astype(jnp.float32),
        lax.psum_scatter(
            grad_wdown.astype(jnp.bfloat16), ("shard", "context"), scatter_dimension=0, tiled=True
        ).astype(jnp.float32),
        lax.psum_scatter(
            grad_gattn.astype(jnp.bfloat16), ("shard", "context"), scatter_dimension=0, tiled=True
        ).astype(jnp.float32),
        lax.psum_scatter(
            grad_gmlp.astype(jnp.bfloat16), ("shard", "context"), scatter_dimension=0, tiled=True
        ).astype(jnp.float32),
    )
    return (
        result.reshape(1, rows, width),
        grad_x_part.reshape(1, rows, width),
        reduced[0],
        reduced[1],
        reduced[2],
        reduced[3],
        reduced[4],
        reduced[5],
        reduced[6],
        reduced[7],
        reduced[8],
    )


def solution(mesh):
    placed = (
        P("shard", "context", None),
        P("shard", "context"),
        P("shard", "context"),
        P(("shard", "context"), "tensor"),
        P(("shard", "context"), "tensor"),
        P(("shard", "context"), "tensor"),
        P(("shard", "context"), "tensor"),
        P(("shard", "context"), "tensor"),
        P(("shard", "context"), "tensor"),
        P(("shard", "context"), "tensor"),
        P(("shard", "context")),
        P(("shard", "context")),
        P("shard", "context", None),
    )
    return jax.shard_map(
        on_device,
        mesh=mesh,
        in_specs=placed,
        out_specs=(
            P("shard", "context", None),
            P("shard", "context", None),
            P(("shard", "context"), "tensor"),
            P(("shard", "context"), "tensor"),
            P(("shard", "context"), "tensor"),
            P(("shard", "context"), "tensor"),
            P(("shard", "context"), "tensor"),
            P(("shard", "context"), "tensor"),
            P(("shard", "context"), "tensor"),
            P(("shard", "context")),
            P(("shard", "context")),
        ),
        check_vma=False,
    )
```

profile of v0, /device:TPU:0, one launch (start us, length us, event | category | flops | bytes accessed | tf_op | source)
XLA Modules:
  0.0 1685.4 jit_solution(14790218301723463259)
XLA Ops:
  16.6 18.3 %all-gather = bf16[8,1,256]{2,1,0:T(2,128)(2,1)S(1)} all-gather(bf16[1,1,256]{2,1,0:T(2,128)(2,1)S(1)} %reshape.451), channel_id=1, replica_groups=mesh['shard'=2,'context'=4,'tensor'=4] {'shard','context'}, dimensions={0}, use_global_device_ids=true | all-gather | bytes 4608 | tf_op jit(solution)/shard_map/all_gather | solution.py:153
  46.8 25.0 %all-gather.10.cloned.1.call-done = bf16[2048,512]{1,0:T(8,128)(2,1)} async-done(((bf16[256,512]{1,0:T(8,128)(2,1)}), bf16[2048,512]{1,0:T(8,128)(2,1)}) %all-gather.10.cloned.1.call-update) | async-done | bytes 2097168 | tf_op jit(solution)/shard_map/all_gather | solution.py:147
  80.5 21.5 %all-gather.14.cloned.1.call-done = bf16[2048,512]{1,0:T(8,128)(2,1)} async-done(((bf16[256,512]{1,0:T(8,128)(2,1)}), bf16[2048,512]{1,0:T(8,128)(2,1)}) %all-gather.14.cloned.1.call-update) | async-done | bytes 2097168 | tf_op jit(solution)/shard_map/all_gather | solution.py:146
  117.3 105.5 %while.44 = (s32[]{:T(128)}, bf16[512,512]{0,1:T(8,128)(2,1)}, bf16[512,512]{0,1:T(8,128)(2,1)}, s32[512]{0:T(512)S(1)}, s32[512]{0:T(512)S(1)}, /*index=5*/f32[...) while((s32[]{:T(128)}, bf16[512,512]{0,1:T(8,128)(2,1)}, ...), condition=%wide.region_6.7_spmd, body=%wide.region_3.6_spmd.sunk | while | flops 565452800 | bytes 44859724 | solution.py:192
  122.5 20.8 %collective-permute-done.3 = s32[512]{0:T(512)S(1)} collective-permute-done((s32[512]{0:T(512)S(1)}, s32[512]{0:T(512)S(1)}, u32[]{:S(2)}, u32[]{:S(2)}) %collective-permute-start.3) | collective-permute-done | bytes 2080 | tf_op jit(solution)/shard_map/while/body/eval_jaxpr/ppermute | solution.py:16
  164.3 12.0 collective-permute-done.3
  196.5 12.0 collective-permute-done.3
  230.8 12.8 all-gather.1
  243.6 52.8 %all-reduce.8.cloned.1.call-done = bf16[512,2048]{1,0:T(8,128)(2,1)} async-done(((bf16[512,2048]{1,0:T(8,128)(2,1)}), bf16[512,2048]{1,0:T(8,128)(2,1)}) %all-reduce.8.cloned.1.call-update) | async-done | bytes 2097168 | tf_op jit(solution)/shard_map/psum | solution.py:71
  301.3 78.6 %all-gather.20.cloned.1.call-done = bf16[2048,2048]{1,0:T(8,128)(2,1)} async-done(((bf16[256,2048]{1,0:T(8,128)(2,1)}), bf16[2048,2048]{1,0:T(8,128)(2,1)}) %all-gather.20.cloned.1.call-update) | async-done | bytes 8388624 | tf_op jit(solution)/shard_map/all_gather | solution.py:151
  379.9 10.6 fusion.91
  390.5 71.6 %all-gather.18.cloned.1.call-done = bf16[2048,2048]{1,0:T(8,128)(2,1)} async-done(((bf16[256,2048]{1,0:T(8,128)(2,1)}), bf16[2048,2048]{1,0:T(8,128)(2,1)}) %all-gather.18.cloned.1.call-update) | async-done | bytes 8388624 | tf_op jit(solution)/shard_map/all_gather | solution.py:150
  462.1 10.6 fusion.90
  472.7 71.6 %all-gather.22.cloned.1.call-done = bf16[2048,2048]{1,0:T(8,128)(2,1)} async-done(((bf16[256,2048]{1,0:T(8,128)(2,1)}), bf16[2048,2048]{1,0:T(8,128)(2,1)}) %all-gather.22.cloned.1.call-update) | async-done | bytes 8388624 | tf_op jit(solution)/shard_map/all_gather | solution.py:152
  544.3 14.1 multiply_convert_fusion.2
  572.4 67.9 %all-reduce.10.cloned.1.call-done = bf16[512,2048]{1,0:T(8,128)(2,1)} async-done(((bf16[512,2048]{1,0:T(8,128)(2,1)}), bf16[512,2048]{1,0:T(8,128)(2,1)}) %all-reduce.10.cloned.1.call-update) | async-done | bytes 2097168 | tf_op jit(solution)/shard_map/psum | solution.py:75
  665.3 227.0 %while.45 = (s32[]{:T(128)}, bf16[512,512]{0,1:T(8,128)(2,1)}, bf16[512,512]{0,1:T(8,128)(2,1)}, s32[512]{0:T(512)S(1)}, s32[512]{0:T(512)S(1)}, /*index=5*/f32[...) while((s32[]{:T(128)}, bf16[512,512]{0,1:T(8,128)(2,1)}, ...), condition=%wide.region_14.15_spmd, body=%wide.region_13.14_spmd.sunk | while | flops 1372061696 | bytes 71647696 | solution.py:265
  671.8 17.6 %collective-permute-done.7 = s32[512]{0:T(512)S(1)} collective-permute-done((s32[512]{0:T(512)S(1)}, s32[512]{0:T(512)S(1)}, u32[]{:S(2)}, u32[]{:S(2)}) %collective-permute-start.7) | collective-permute-done | bytes 2080 | tf_op jit(solution)/shard_map/while/body/eval_jaxpr/ppermute | solution.py:16
  692.6 61.4 %collective-permute-done.5 = bf16[512,512]{0,1:T(8,128)(2,1)S(1)} collective-permute-done((bf16[512,512]{0,1:T(8,128)(2,1)}, bf16[512,512]{0,1:T(8,128)(2,1)S(1)}, u32[]{:S(2)}, u32[]{:S(2)}) %collective-permute-start.5) | collective-permute-done | bytes 524320 | tf_op jit(solution)/shard_map/while/body/eval_jaxpr/ppermute | solution.py:16
  773.6 11.9 collective-permute-done.7
  787.2 29.1 %collective-permute-done.5 = bf16[512,512]{0,1:T(8,128)(2,1)S(1)} collective-permute-done((bf16[512,512]{0,1:T(8,128)(2,1)}, bf16[512,512]{0,1:T(8,128)(2,1)S(1)}, u32[]{:S(2)}, u32[]{:S(2)}) %collective-permute-start.5) | collective-permute-done | bytes 524320 | tf_op jit(solution)/shard_map/while/body/eval_jaxpr/ppermute | solution.py:16
  835.9 11.9 collective-permute-done.7
  849.4 28.2 %collective-permute-done.5 = bf16[512,512]{0,1:T(8,128)(2,1)S(1)} collective-permute-done((bf16[512,512]{0,1:T(8,128)(2,1)}, bf16[512,512]{0,1:T(8,128)(2,1)S(1)}, u32[]{:S(2)}, u32[]{:S(2)}) %collective-permute-start.5) | collective-permute-done | bytes 524320 | tf_op jit(solution)/shard_map/while/body/eval_jaxpr/ppermute | solution.py:16
  892.4 12.1 collective-permute-done.11
  908.1 19.6 %collective-permute-done.10 = bf16[512,512]{0,1:T(8,128)(2,1)S(1)} collective-permute-done((bf16[512,512]{0,1:T(8,128)(2,1)}, bf16[512,512]{0,1:T(8,128)(2,1)S(1)}, u32[]{:S(2)}, u32[]{:S(2)}) %collective-permute-start.10) | collective-permute-done | bytes 524320 | tf_op jit(solution)/shard_map/ppermute | solution.py:16
  987.0 21.2 %reduce-scatter.10.cloned.1.call-done = bf16[256,512]{1,0:T(8,128)(2,1)} async-done(((bf16[2048,512]{1,0:T(8,128)(2,1)}), bf16[256,512]{1,0:T(8,128)(2,1)}) %reduce-scatter.10.cloned.1.call-update) | async-done | bytes 262160 | tf_op jit(solution)/shard_map/reduce_scatter | solution.py:299
  1009.9 49.3 %reduce-scatter.8.cloned.1.call-done = bf16[256,512]{1,0:T(8,128)(2,1)} async-done(((bf16[2048,512]{1,0:T(8,128)(2,1)}), bf16[256,512]{1,0:T(8,128)(2,1)}) %reduce-scatter.8.cloned.1.call-update) | async-done | bytes 262160 | tf_op jit(solution)/shard_map/reduce_scatter | solution.py:296
  1061.1 105.0 %all-reduce.12.cloned.1.call-done = (bf16[512,2048]{1,0:T(8,128)(2,1)}, bf16[512,2048]{1,0:T(8,128)(2,1)}) async-done(((bf16[512,2048]{1,0:T(8,128)(2,1)}, bf16[512,2048]{1,0:T(8,128)(2,1)}), (bf16[512,2048]{1,0:T(8,128)(2,1)}, bf16[512,2048]{1,0:T(8,128)(2,1)})) %all-reduce.12.cloned.1.call-update) | async-done | bytes 4194320 | tf_op jit(solution)/shard_map/psum | solution.py:71
  1168.9 19.6 %all-reduce.2 = (bf16[2048]{0:T(1024)(128)(2,1)S(1)}, bf16[2048]{0:T(1024)(128)(2,1)S(1)}) all-reduce(bf16[2048]{0:T(1024)(128)(2,1)S(1)} %get-tuple-element.174, bf16[2048]{0:T(1024)(128)(2,1)S(1)} %copy-done.44), channel_id=9, replica_groups=mesh['shard'=2,'context'=4,'tensor'=4] {'shard','context'}, use_global_device_ids=true, to_apply=%region_25.26.clone | all-reduce | flops 4096 | bytes 16384
  1197.9 137.8 %reduce-scatter.20.cloned.1.call-done = bf16[256,2048]{0,1:T(8,128)(2,1)} async-done(((bf16[2048,2048]{0,1:T(8,128)(2,1)}), bf16[256,2048]{0,1:T(8,128)(2,1)}) %reduce-scatter.20.cloned.1.call-update) | async-done | bytes 1048592 | tf_op jit(solution)/shard_map/reduce_scatter | solution.py:314
  1338.3 167.5 %reduce-scatter.18.cloned.1.call-done = bf16[256,2048]{1,0:T(8,128)(2,1)} async-done(((bf16[2048,2048]{1,0:T(8,128)(2,1)}), bf16[256,2048]{1,0:T(8,128)(2,1)}) %reduce-scatter.18.cloned.1.call-update) | async-done | bytes 1048592 | tf_op jit(solution)/shard_map/reduce_scatter | solution.py:311
  1508.6 167.3 %reduce-scatter.16.cloned.1.call-done = bf16[256,2048]{1,0:T(8,128)(2,1)} async-done(((bf16[2048,2048]{1,0:T(8,128)(2,1)}), bf16[256,2048]{1,0:T(8,128)(2,1)}) %reduce-scatter.16.cloned.1.call-update) | async-done | bytes 1048592 | tf_op jit(solution)/shard_map/reduce_scatter | solution.py:308
  (365 shorter events, 309.8 us)
Async XLA Ops:
  7.2 34.5 %all-gather.12.cloned.1.call-start = ((), (), s32[]{:S(2)}) async-start(), calls=%async_computation.8 | async-start | bytes 2359296 | tf_op jit(solution)/shard_map/all_gather | solution.py:148
  7.9 63.9 %all-gather.10.cloned.1.call-start = ((), (), s32[]{:S(2)}) async-start(), calls=%async_computation.7 | async-start | bytes 2359296 | tf_op jit(solution)/shard_map/all_gather | solution.py:147
  8.7 93.3 %all-gather.14.cloned.1.call-start = ((), (), s32[]{:S(2)}) async-start(), calls=%async_computation.9 | async-start | bytes 2359296 | tf_op jit(solution)/shard_map/all_gather | solution.py:146
  9.4 214.8 %all-gather.16.cloned.1.call-start = ((), (), s32[]{:S(2)}) async-start(), calls=%async_computation.10 | async-start | bytes 2359296 | tf_op jit(solution)/shard_map/all_gather | solution.py:149
  10.0 286.5 %all-reduce.8.cloned.1.call-start = ((), (), s32[]{:S(2)}) async-start(), calls=%async_computation.11 | async-start | bytes 4194304 | tf_op jit(solution)/shard_map/psum | solution.py:71
  117.5 26.1 %collective-permute-start = (bf16[512,512]{0,1:T(8,128)(2,1)}, bf16[512,512]{0,1:T(8,128)(2,1)}, u32[]{:S(2)}, u32[]{:S(2)}) collective-permute-start(bf16[512,512]{0,1:T(8,128)(2,1)} %get-tuple-element.432), channel_id=1, source_target_pairs={{0,4},{4,8},{8,12},{12,0},{1,5},{5,9},{9,13},{13,1},{2,6},{6,10},{... | collective-permute-start | bytes 1572872 | tf_op jit(solution)/shard_map/while/body/eval_jaxpr/ppermute | solution.py:16
  119.0 24.3 %collective-permute-start.3 = (s32[512]{0:T(512)S(1)}, s32[512]{0:T(512)S(1)}, u32[]{:S(2)}, u32[]{:S(2)}) collective-permute-start(s32[512]{0:T(512)S(1)} %get-tuple-element.435), channel_id=1, source_target_pairs={{0,4},{4,8},{8,12},{12,0},{1,5},{5,9},{9,13},{13,1},{2,6},{6,10},{... | collective-permute-start | bytes 6152 | tf_op jit(solution)/shard_map/while/body/eval_jaxpr/ppermute | solution.py:16
  120.5 33.8 %collective-permute-start.1 = (bf16[512,512]{0,1:T(8,128)(2,1)}, bf16[512,512]{0,1:T(8,128)(2,1)S(1)}, u32[]{:S(2)}, u32[]{:S(2)}) collective-permute-start(bf16[512,512]{0,1:T(8,128)(2,1)} %get-tuple-element.433), channel_id=1, source_target_pairs={{0,4},{4,8},{8,12},{12,0},{1,5},{5,9},{9,13},{13,1},{2,6},{6,10},{... | collective-permute-start | bytes 1572872 | tf_op jit(solution)/shard_map/while/body/eval_jaxpr/ppermute | solution.py:16
  161.1 25.4 %collective-permute-start.1 = (bf16[512,512]{0,1:T(8,128)(2,1)}, bf16[512,512]{0,1:T(8,128)(2,1)S(1)}, u32[]{:S(2)}, u32[]{:S(2)}) collective-permute-start(bf16[512,512]{0,1:T(8,128)(2,1)} %get-tuple-element.433), channel_id=1, source_target_pairs={{0,4},{4,8},{8,12},{12,0},{1,5},{5,9},{9,13},{13,1},{2,6},{6,10},{... | collective-permute-start | bytes 1572872 | tf_op jit(solution)/shard_map/while/body/eval_jaxpr/ppermute | solution.py:16
  192.3 25.4 %collective-permute-start.1 = (bf16[512,512]{0,1:T(8,128)(2,1)}, bf16[512,512]{0,1:T(8,128)(2,1)S(1)}, u32[]{:S(2)}, u32[]{:S(2)}) collective-permute-start(bf16[512,512]{0,1:T(8,128)(2,1)} %get-tuple-element.433), channel_id=1, source_target_pairs={{0,4},{4,8},{8,12},{12,0},{1,5},{5,9},{9,13},{13,1},{2,6},{6,10},{... | collective-permute-start | bytes 1572872 | tf_op jit(solution)/shard_map/while/body/eval_jaxpr/ppermute | solution.py:16
  228.6 151.3 %all-gather.20.cloned.1.call-start = ((), (), s32[]{:S(2)}) async-start(), calls=%async_computation.13 | async-start | bytes 9437184 | tf_op jit(solution)/shard_map/all_gather | solution.py:151
  229.2 232.9 %all-gather.18.cloned.1.call-start = ((), (), s32[]{:S(2)}) async-start(), calls=%async_computation.12 | async-start | bytes 9437184 | tf_op jit(solution)/shard_map/all_gather | solution.py:150
  230.0 314.3 %all-gather.22.cloned.1.call-start = ((), (), s32[]{:S(2)}) async-start(), calls=%async_computation.14 | async-start | bytes 9437184 | tf_op jit(solution)/shard_map/all_gather | solution.py:152
  230.7 409.5 %all-reduce.10.cloned.1.call-start = ((), (), s32[]{:S(2)}) async-start(), calls=%async_computation.15 | async-start | bytes 4194304 | tf_op jit(solution)/shard_map/psum | solution.py:75
  572.1 411.2 %reduce-scatter.14.cloned.1.call-start = ((), (), s32[]{:S(2)}) async-start(), calls=%async_computation.19 | async-start | bytes 2359296 | tf_op jit(solution)/shard_map/reduce_scatter | solution.py:305
  665.0 320.2 %reduce-scatter.12.cloned.1.call-start = ((), (), s32[]{:S(2)}) async-start(), calls=%async_computation.18 | async-start | bytes 2359296 | tf_op jit(solution)/shard_map/reduce_scatter | solution.py:302
  665.3 26.0 %collective-permute-start.4 = (bf16[512,512]{0,1:T(8,128)(2,1)}, bf16[512,512]{0,1:T(8,128)(2,1)S(1)}, u32[]{:S(2)}, u32[]{:S(2)}) collective-permute-start(bf16[512,512]{0,1:T(8,128)(2,1)} %get-tuple-element.471), channel_id=1, source_target_pairs={{0,4},{4,8},{8,12},{12,0},{1,5},{5,9},{9,13},{13,1},{2,6},{6,10},{... | collective-permute-start | bytes 1572872 | tf_op jit(solution)/shard_map/while/body/eval_jaxpr/ppermute | solution.py:16
  669.8 91.5 %collective-permute-start.9 = (bf16[512,512]{0,1:T(8,128)(2,1)}, bf16[512,512]{0,1:T(8,128)(2,1)}, u32[]{:S(2)}, u32[]{:S(2)}) collective-permute-start(bf16[512,512]{0,1:T(8,128)(2,1)} %get-tuple-element.477), channel_id=1, source_target_pairs={{0,4},{4,8},{8,12},{12,0},{1,5},{5,9},{9,13},{13,1},{2,6},{6,10},{... | collective-permute-start | bytes 1572872 | tf_op jit(solution)/shard_map/while/body/eval_jaxpr/ppermute | solution.py:16
  670.3 96.0 %collective-permute-start.8 = (bf16[512,512]{0,1:T(8,128)(2,1)}, bf16[512,512]{0,1:T(8,128)(2,1)}, u32[]{:S(2)}, u32[]{:S(2)}) collective-permute-start(bf16[512,512]{0,1:T(8,128)(2,1)} %get-tuple-element.476), channel_id=1, source_target_pairs={{0,4},{4,8},{8,12},{12,0},{1,5},{5,9},{9,13},{13,1},{2,6},{6,10},{... | collective-permute-start | bytes 1572872 | tf_op jit(solution)/shard_map/while/body/eval_jaxpr/ppermute | solution.py:16
  689.4 64.6 %collective-permute-start.5 = (bf16[512,512]{0,1:T(8,128)(2,1)}, bf16[512,512]{0,1:T(8,128)(2,1)S(1)}, u32[]{:S(2)}, u32[]{:S(2)}) collective-permute-start(bf16[512,512]{0,1:T(8,128)(2,1)} %get-tuple-element.472), channel_id=1, source_target_pairs={{0,4},{4,8},{8,12},{12,0},{1,5},{5,9},{9,13},{13,1},{2,6},{6,10},{... | collective-permute-start | bytes 1572872 | tf_op jit(solution)/shard_map/while/body/eval_jaxpr/ppermute | solution.py:16
  771.3 52.2 %collective-permute-start.9 = (bf16[512,512]{0,1:T(8,128)(2,1)}, bf16[512,512]{0,1:T(8,128)(2,1)}, u32[]{:S(2)}, u32[]{:S(2)}) collective-permute-start(bf16[512,512]{0,1:T(8,128)(2,1)} %get-tuple-element.477), channel_id=1, source_target_pairs={{0,4},{4,8},{8,12},{12,0},{1,5},{5,9},{9,13},{13,1},{2,6},{6,10},{... | collective-permute-start | bytes 1572872 | tf_op jit(solution)/shard_map/while/body/eval_jaxpr/ppermute | solution.py:16
  773.6 54.9 %collective-permute-start.8 = (bf16[512,512]{0,1:T(8,128)(2,1)}, bf16[512,512]{0,1:T(8,128)(2,1)}, u32[]{:S(2)}, u32[]{:S(2)}) collective-permute-start(bf16[512,512]{0,1:T(8,128)(2,1)} %get-tuple-element.476), channel_id=1, source_target_pairs={{0,4},{4,8},{8,12},{12,0},{1,5},{5,9},{9,13},{13,1},{2,6},{6,10},{... | collective-permute-start | bytes 1572872 | tf_op jit(solution)/shard_map/while/body/eval_jaxpr/ppermute | solution.py:16
  785.5 30.7 %collective-permute-start.5 = (bf16[512,512]{0,1:T(8,128)(2,1)}, bf16[512,512]{0,1:T(8,128)(2,1)S(1)}, u32[]{:S(2)}, u32[]{:S(2)}) collective-permute-start(bf16[512,512]{0,1:T(8,128)(2,1)} %get-tuple-element.472), channel_id=1, source_target_pairs={{0,4},{4,8},{8,12},{12,0},{1,5},{5,9},{9,13},{13,1},{2,6},{6,10},{... | collective-permute-start | bytes 1572872 | tf_op jit(solution)/shard_map/while/body/eval_jaxpr/ppermute | solution.py:16
  832.6 52.3 %collective-permute-start.9 = (bf16[512,512]{0,1:T(8,128)(2,1)}, bf16[512,512]{0,1:T(8,128)(2,1)}, u32[]{:S(2)}, u32[]{:S(2)}) collective-permute-start(bf16[512,512]{0,1:T(8,128)(2,1)} %get-tuple-element.477), channel_id=1, source_target_pairs={{0,4},{4,8},{8,12},{12,0},{1,5},{5,9},{9,13},{13,1},{2,6},{6,10},{... | collective-permute-start | bytes 1572872 | tf_op jit(solution)/shard_map/while/body/eval_jaxpr/ppermute | solution.py:16
  835.9 54.1 %collective-permute-start.8 = (bf16[512,512]{0,1:T(8,128)(2,1)}, bf16[512,512]{0,1:T(8,128)(2,1)}, u32[]{:S(2)}, u32[]{:S(2)}) collective-permute-start(bf16[512,512]{0,1:T(8,128)(2,1)} %get-tuple-element.476), channel_id=1, source_target_pairs={{0,4},{4,8},{8,12},{12,0},{1,5},{5,9},{9,13},{13,1},{2,6},{6,10},{... | collective-permute-start | bytes 1572872 | tf_op jit(solution)/shard_map/while/body/eval_jaxpr/ppermute | solution.py:16
  847.8 29.9 %collective-permute-start.5 = (bf16[512,512]{0,1:T(8,128)(2,1)}, bf16[512,512]{0,1:T(8,128)(2,1)S(1)}, u32[]{:S(2)}, u32[]{:S(2)}) collective-permute-start(bf16[512,512]{0,1:T(8,128)(2,1)} %get-tuple-element.472), channel_id=1, source_target_pairs={{0,4},{4,8},{8,12},{12,0},{1,5},{5,9},{9,13},{13,1},{2,6},{6,10},{... | collective-permute-start | bytes 1572872 | tf_op jit(solution)/shard_map/while/body/eval_jaxpr/ppermute | solution.py:16
  908.0 100.1 %reduce-scatter.10.cloned.1.call-start = ((), (), s32[]{:S(2)}) async-start(), calls=%async_computation.17 | async-start | bytes 2359296 | tf_op jit(solution)/shard_map/reduce_scatter | solution.py:299
  931.1 128.1 %reduce-scatter.8.cloned.1.call-start = ((), (), s32[]{:S(2)}) async-start(), calls=%async_computation.16 | async-start | bytes 2359296 | tf_op jit(solution)/shard_map/reduce_scatter | solution.py:296
  934.0 232.0 %all-reduce.12.cloned.1.call-start = ((), (), s32[]{:S(2)}) async-start(), calls=%async_computation.23 | async-start | bytes 8388608 | tf_op jit(solution)/shard_map/psum | solution.py:71
  950.5 385.3 %reduce-scatter.20.cloned.1.call-start = ((), (), s32[]{:S(2)}) async-start(), calls=%async_computation.22 | async-start | bytes 9437184 | tf_op jit(solution)/shard_map/reduce_scatter | solution.py:314
  960.8 544.9 %reduce-scatter.18.cloned.1.call-start = ((), (), s32[]{:S(2)}) async-start(), calls=%async_computation.21 | async-start | bytes 9437184 | tf_op jit(solution)/shard_map/reduce_scatter | solution.py:311
  971.0 704.8 %reduce-scatter.16.cloned.1.call-start = ((), (), s32[]{:S(2)}) async-start(), calls=%async_computation.20 | async-start | bytes 9437184 | tf_op jit(solution)/shard_map/reduce_scatter | solution.py:308
  (83 other events, 3145.1 us)
Sparse Core Ops, SparseCore 0:
  9.6 32.0 all-gather.11
  43.2 28.5 all-gather.9
  73.4 28.5 all-gather.13
  103.4 36.3 all-gather.15
  228.8 67.6 all-reduce.7
  297.9 82.0 all-gather.19
  381.5 80.5 all-gather.17
  463.7 80.5 all-gather.21
  572.2 67.9 all-reduce.9
  665.1 88.9 reduce-scatter.13
  908.1 51.4 reduce-scatter.11
  961.8 46.2 reduce-scatter.9
  1011.0 48.2 reduce-scatter.7
  1063.2 102.8 all-reduce.11
  1168.2 167.5 reduce-scatter.19
  1337.9 167.8 reduce-scatter.17
  1507.9 167.8 reduce-scatter.15
where the time goes:
time: 1690 us
  waiting for transfers between devices  1300 us (77%)
  matrix products  186 us (11%)
  other arithmetic  64.5 us (4%)
  blocking collectives  50.7 us (3%)
  starting transfers between devices  34.9 us (2%)
  local copies, waits for them, and re-layouts  32.6 us (2%)
    ppermute x32, waiting for transfers between devices, passed_along(): return lax.ppermute(value, axis, pairs)  252 us
    reduce_scatter x1, waiting for transfers between devices, on_device(): lax.psum_scatter(grad_wup.astype(jnp.bfloat16), ('shard', 'context'), sca...  167 us
    reduce_scatter x1, waiting for transfers between devices, on_device(): lax.psum_scatter(grad_wgate.astype(jnp.bfloat16), ('shard', 'context'), s...  167 us
    psum x2, waiting for transfers between devices, branch_total(): lax.psum(partial_sum.astype(jnp.bfloat16), 'tensor').astype(jnp.float32)  158 us
    reduce_scatter x1, waiting for transfers between devices, on_device(): lax.psum_scatter(grad_wdown.astype(jnp.bfloat16), ('shard', 'context'), s...  138 us
    all_gather x1, waiting for transfers between devices, on_device(): lax.all_gather(w_up, ('shard', 'context'), axis=0, tiled=True)  78.6 us
    all_gather x1, waiting for transfers between devices, on_device(): lax.all_gather(w_gate, ('shard', 'context'), axis=0, tiled=True)  71.6 us
    all_gather x1, waiting for transfers between devices, on_device(): lax.all_gather(w_down, ('shard', 'context'), axis=0, tiled=True)  71.6 us
  transfers between devices with their start and end apart: 49, of which 28 were waited for; matrix products, arithmetic and copies ran while one was open for 13% of the time, Pallas kernels for 0%

commit v1 on v0

--- a/solution.py
+++ b/solution.py
@@ -72,7 +72,9 @@
 
 
 def input_total(partial_sum):
-    return lax.psum(partial_sum.astype(jnp.bfloat16), "tensor").astype(jnp.float32)
+    return jnp.sum(lax.all_gather(partial_sum.astype(jnp.bfloat16), "tensor"), axis=0).astype(
+        jnp.float32
+    )
 
 
 def pass_grads(grad_key, grad_value):

time: 1690 us -> 1730 us (1.024)
  starting transfers between devices: 34.9 us -> 140 us
  waiting for transfers between devices: 1300 us -> 1210 us
    all_gather x0 -> x2, waiting for transfers between devices: none -> 173 us  [input_total(): lax.all_gather(partial_sum.astype(jnp.bfloat16), 'tensor')]
    reduce_scatter x1, waiting for transfers between devices: 167 us -> 0.01 us  [on_device(): lax.psum_scatter(grad_wup.astype(jnp.bfloat16), ('shard', 'context'), sca...]
    reduce_scatter x1, waiting for transfers between devices: 138 us -> 0.01 us  [on_device(): lax.psum_scatter(grad_wdown.astype(jnp.bfloat16), ('shard', 'context'), s...]
    ppermute x32, starting transfers between devices: 33 us -> 139 us  [passed_along(): return lax.ppermute(value, axis, pairs)]
    ppermute x32, waiting for transfers between devices: 252 us -> 356 us  [passed_along(): return lax.ppermute(value, axis, pairs)]
    psum x1 -> x0, waiting for transfers between devices: 67.9 us -> none  [input_total(): lax.psum(partial_sum.astype(jnp.bfloat16), 'tensor').astype(jnp.float32)]
    psum x2, waiting for transfers between devices: 158 us -> 97.2 us  [branch_total(): lax.psum(partial_sum.astype(jnp.bfloat16), 'tensor').astype(jnp.float32)]
    reduce_scatter x1, waiting for transfers between devices: 0.01 us -> 49.7 us  [on_device(): lax.psum_scatter(grad_wv.astype(jnp.bfloat16), ('shard', 'context'), scat...]
  transfers between devices with their start and end apart: 49 -> 50, of which waited for: 28 -> 28; matrix products, arithmetic and copies ran while one was open for 13% -> 14% of each run, Pallas kernels for 0% -> 0%
where the time goes in v1:
time: 1730 us; the launch traced here: 1720 us
  waiting for transfers between devices  1210 us (70%)
  matrix products  203 us (12%)
  starting transfers between devices  140 us (8%)
  other arithmetic  79.8 us (5%)
  blocking collectives  47.3 us (3%)
  local copies, waits for them, and re-layouts  31 us (2%)
    ppermute x32, waiting for transfers between devices, passed_along(): return lax.ppermute(value, axis, pairs)  356 us
    all_gather x2, waiting for transfers between devices, input_total(): lax.all_gather(partial_sum.astype(jnp.bfloat16), 'tensor')  173 us
    reduce_scatter x1, waiting for transfers between devices, on_device(): lax.psum_scatter(grad_wgate.astype(jnp.bfloat16), ('shard', 'context'), s...  151 us
    ppermute x32, starting transfers between devices, passed_along(): return lax.ppermute(value, axis, pairs)  139 us
    psum x2, waiting for transfers between devices, branch_total(): lax.psum(partial_sum.astype(jnp.bfloat16), 'tensor').astype(jnp.float32)  97.2 us
    all_gather x1, waiting for transfers between devices, on_device(): lax.all_gather(w_up, ('shard', 'context'), axis=0, tiled=True)  78.6 us
    all_gather x1, waiting for transfers between devices, on_device(): lax.all_gather(w_gate, ('shard', 'context'), axis=0, tiled=True)  71.6 us
    all_gather x1, waiting for transfers between devices, on_device(): lax.all_gather(w_down, ('shard', 'context'), axis=0, tiled=True)  71.6 us
  transfers between devices with their start and end apart: 50, of which 28 were waited for; matrix products, arithmetic and copies ran while one was open for 14% of the time, Pallas kernels for 0%

profile of v1, /device:TPU:0, one launch (start us, length us, event | category | flops | bytes accessed | tf_op | source)
XLA Modules:
  0.0 1723.1 jit_solution(11396122312231476411)
XLA Ops:
  15.9 18.3 %all-gather.2 = bf16[8,1,256]{2,1,0:T(2,128)(2,1)S(1)} all-gather(bf16[1,1,256]{2,1,0:T(2,128)(2,1)S(1)} %reshape.453), channel_id=1, replica_groups=mesh['shard'=2,'context'=4,'tensor'=4] {'shard','context'}, dimensions={0}, use_global_device_ids=true | all-gather | bytes 4608 | tf_op jit(solution)/shard_map/all_gather | solution.py:155
  46.8 25.0 %all-gather.14.cloned.1.call-done = bf16[2048,512]{1,0:T(8,128)(2,1)} async-done(((bf16[256,512]{1,0:T(8,128)(2,1)}), bf16[2048,512]{1,0:T(8,128)(2,1)}) %all-gather.14.cloned.1.call-update) | async-done | bytes 2097168 | tf_op jit(solution)/shard_map/all_gather | solution.py:149
  79.9 22.1 %all-gather.18.cloned.1.call-done = bf16[2048,512]{1,0:T(8,128)(2,1)} async-done(((bf16[256,512]{1,0:T(8,128)(2,1)}), bf16[2048,512]{1,0:T(8,128)(2,1)}) %all-gather.18.cloned.1.call-update) | async-done | bytes 2097168 | tf_op jit(solution)/shard_map/all_gather | solution.py:148
  117.3 105.5 %while.44 = (s32[]{:T(128)}, bf16[512,512]{0,1:T(8,128)(2,1)}, bf16[512,512]{0,1:T(8,128)(2,1)}, s32[512]{0:T(512)S(1)}, s32[512]{0:T(512)S(1)}, /*index=5*/f32[...) while((s32[]{:T(128)}, bf16[512,512]{0,1:T(8,128)(2,1)}, ...), condition=%wide.region_6.7_spmd, body=%wide.region_3.6_spmd.sunk | while | flops 565452800 | bytes 44859724 | solution.py:194
  122.5 20.8 %collective-permute-done.3 = s32[512]{0:T(512)S(1)} collective-permute-done((s32[512]{0:T(512)S(1)}, s32[512]{0:T(512)S(1)}, u32[]{:S(2)}, u32[]{:S(2)}) %collective-permute-start.3) | collective-permute-done | bytes 2080 | tf_op jit(solution)/shard_map/while/body/eval_jaxpr/ppermute | solution.py:16
  230.6 12.8 all-gather.3
  243.4 52.8 %all-reduce.6.cloned.1.call-done = bf16[512,2048]{1,0:T(8,128)(2,1)} async-done(((bf16[512,2048]{1,0:T(8,128)(2,1)}), bf16[512,2048]{1,0:T(8,128)(2,1)}) %all-reduce.6.cloned.1.call-update) | async-done | bytes 2097168 | tf_op jit(solution)/shard_map/psum | solution.py:71
  301.1 78.6 %all-gather.24.cloned.1.call-done = bf16[2048,2048]{1,0:T(8,128)(2,1)} async-done(((bf16[256,2048]{1,0:T(8,128)(2,1)}), bf16[2048,2048]{1,0:T(8,128)(2,1)}) %all-gather.24.cloned.1.call-update) | async-done | bytes 8388624 | tf_op jit(solution)/shard_map/all_gather | solution.py:153
  390.3 71.6 %all-gather.22.cloned.1.call-done = bf16[2048,2048]{1,0:T(8,128)(2,1)} async-done(((bf16[256,2048]{1,0:T(8,128)(2,1)}), bf16[2048,2048]{1,0:T(8,128)(2,1)}) %all-gather.22.cloned.1.call-update) | async-done | bytes 8388624 | tf_op jit(solution)/shard_map/all_gather | solution.py:152
  472.5 71.6 %all-gather.26.cloned.1.call-done = bf16[2048,2048]{1,0:T(8,128)(2,1)} async-done(((bf16[256,2048]{1,0:T(8,128)(2,1)}), bf16[2048,2048]{1,0:T(8,128)(2,1)}) %all-gather.26.cloned.1.call-update) | async-done | bytes 8388624 | tf_op jit(solution)/shard_map/all_gather | solution.py:154
  544.1 26.0 %multiply_convert_fusion.2 = (bf16[512,2048]{1,0:T(8,128)(2,1)S(1)}, bf16[512,2048]{1,0:T(8,128)(2,1)S(1)}, bf16[512,2048]{1,0:T(8,128)(2,1)}) fusion(f32[512,2048]{1,0:T(8,128)} %fusion.90, f32[512,2048]{1,0:T(8,128)} %fusion.91, bf16[2048,2048]{1,0:T(8,128)(2,1)} %all-gather.26.cloned.1.call-done, bf16[1,512,2048]{2,1,0:T(8,128)(2,1)} %param.29), kind=kOutput, calls=%fused_computation.68 | convolution fusion | flops 4310695936 | bytes 25165824 | tf_op jit(solution)/shard_map/dot_general | solution.py:227
  583.9 86.1 %all-gather.28.cloned.1.call-done = bf16[2048,2048]{1,0:T(8,128)(2,1)} async-done(((bf16[512,2048]{1,0:T(8,128)(2,1)}), bf16[2048,2048]{1,0:T(8,128)(2,1)}) %all-gather.28.cloned.1.call-update) | async-done | bytes 8388624 | tf_op jit(solution)/shard_map/all_gather | solution.py:75
  736.3 370.6 %while.45 = (s32[]{:T(128)}, bf16[512,512]{0,1:T(8,128)(2,1)}, bf16[512,512]{0,1:T(8,128)(2,1)}, s32[512]{0:T(512)S(1)}, s32[512]{0:T(512)S(1)}, /*index=5*/f32[...) while((s32[]{:T(128)}, bf16[512,512]{0,1:T(8,128)(2,1)}, ...), condition=%wide.region_14.15_spmd, body=%wide.region_13.14_spmd.sunk | while | flops 1372061696 | bytes 71647696 | solution.py:267
  742.7 17.3 %collective-permute-done.7 = s32[512]{0:T(512)S(1)} collective-permute-done((s32[512]{0:T(512)S(1)}, s32[512]{0:T(512)S(1)}, u32[]{:S(2)}, u32[]{:S(2)}) %collective-permute-start.7) | collective-permute-done | bytes 2080 | tf_op jit(solution)/shard_map/while/body/eval_jaxpr/ppermute | solution.py:16
  764.7 61.5 %collective-permute-done.5 = bf16[512,512]{0,1:T(8,128)(2,1)S(1)} collective-permute-done((bf16[512,512]{0,1:T(8,128)(2,1)}, bf16[512,512]{0,1:T(8,128)(2,1)S(1)}, u32[]{:S(2)}, u32[]{:S(2)}) %collective-permute-start.5) | collective-permute-done | bytes 524320 | tf_op jit(solution)/shard_map/while/body/eval_jaxpr/ppermute | solution.py:16
  840.9 27.5 %collective-permute-start.4 = (bf16[512,512]{0,1:T(8,128)(2,1)}, bf16[512,512]{0,1:T(8,128)(2,1)S(1)}, u32[]{:S(2)}, u32[]{:S(2)}) collective-permute-start(bf16[512,512]{0,1:T(8,128)(2,1)} %get-tuple-element.469), channel_id=1, source_target_pairs={{0,4},{4,8},{8,12},{12,0},{1,5},{5,9},{9,13},{13,1},{2,6},{6,10},{... | collective-permute-start | bytes 1572872 | tf_op jit(solution)/shard_map/while/body/eval_jaxpr/ppermute | solution.py:16
  873.3 23.0 %collective-permute-done.7 = s32[512]{0:T(512)S(1)} collective-permute-done((s32[512]{0:T(512)S(1)}, s32[512]{0:T(512)S(1)}, u32[]{:S(2)}, u32[]{:S(2)}) %collective-permute-start.7) | collective-permute-done | bytes 2080 | tf_op jit(solution)/shard_map/while/body/eval_jaxpr/ppermute | solution.py:16
  902.6 58.8 %collective-permute-done.5 = bf16[512,512]{0,1:T(8,128)(2,1)S(1)} collective-permute-done((bf16[512,512]{0,1:T(8,128)(2,1)}, bf16[512,512]{0,1:T(8,128)(2,1)S(1)}, u32[]{:S(2)}, u32[]{:S(2)}) %collective-permute-start.5) | collective-permute-done | bytes 524320 | tf_op jit(solution)/shard_map/while/body/eval_jaxpr/ppermute | solution.py:16
  976.1 22.5 %collective-permute-start.4 = (bf16[512,512]{0,1:T(8,128)(2,1)}, bf16[512,512]{0,1:T(8,128)(2,1)S(1)}, u32[]{:S(2)}, u32[]{:S(2)}) collective-permute-start(bf16[512,512]{0,1:T(8,128)(2,1)} %get-tuple-element.469), channel_id=1, source_target_pairs={{0,4},{4,8},{8,12},{12,0},{1,5},{5,9},{9,13},{13,1},{2,6},{6,10},{... | collective-permute-start | bytes 1572872 | tf_op jit(solution)/shard_map/while/body/eval_jaxpr/ppermute | solution.py:16
  1003.6 22.2 %collective-permute-done.7 = s32[512]{0:T(512)S(1)} collective-permute-done((s32[512]{0:T(512)S(1)}, s32[512]{0:T(512)S(1)}, u32[]{:S(2)}, u32[]{:S(2)}) %collective-permute-start.7) | collective-permute-done | bytes 2080 | tf_op jit(solution)/shard_map/while/body/eval_jaxpr/ppermute | solution.py:16
  1034.6 57.7 %collective-permute-done.5 = bf16[512,512]{0,1:T(8,128)(2,1)S(1)} collective-permute-done((bf16[512,512]{0,1:T(8,128)(2,1)}, bf16[512,512]{0,1:T(8,128)(2,1)S(1)}, u32[]{:S(2)}, u32[]{:S(2)}) %collective-permute-start.5) | collective-permute-done | bytes 524320 | tf_op jit(solution)/shard_map/while/body/eval_jaxpr/ppermute | solution.py:16
  1107.0 29.3 %collective-permute-start.11 = (bf16[512,512]{0,1:T(8,128)(2,1)}, bf16[512,512]{0,1:T(8,128)(2,1)S(1)}, u32[]{:S(2)}, u32[]{:S(2)}) collective-permute-start(bf16[512,512]{0,1:T(8,128)(2,1)} %get-tuple-element.149), channel_id=1, source_target_pairs={{0,4},{4,8},{8,12},{12,0},{1,5},{5,9},{9,13},{13,1},{2,6},{6,10},{... | collective-permute-start | bytes 1572872 | tf_op jit(solution)/shard_map/ppermute | solution.py:16
  1136.3 26.6 %collective-permute-done.11 = bf16[512,512]{0,1:T(8,128)(2,1)S(1)} collective-permute-done((bf16[512,512]{0,1:T(8,128)(2,1)}, bf16[512,512]{0,1:T(8,128)(2,1)S(1)}, u32[]{:S(2)}, u32[]{:S(2)}) %collective-permute-start.11) | collective-permute-done | bytes 524320 | tf_op jit(solution)/shard_map/ppermute | solution.py:16
  1166.6 13.0 collective-permute-start.10
  1179.6 28.2 %collective-permute-done.10 = bf16[512,512]{0,1:T(8,128)(2,1)S(1)} collective-permute-done((bf16[512,512]{0,1:T(8,128)(2,1)S(1)}, bf16[512,512]{0,1:T(8,128)(2,1)S(1)}, u32[]{:S(2)}, u32[]{:S(2)}) %collective-permute-start.10) | collective-permute-done | bytes 524320 | tf_op jit(solution)/shard_map/ppermute | solution.py:16
  1241.6 151.4 %reduce-scatter.16.cloned.1.call-done = bf16[256,2048]{1,0:T(8,128)(2,1)} async-done(((bf16[2048,2048]{1,0:T(8,128)(2,1)}), bf16[256,2048]{1,0:T(8,128)(2,1)}) %reduce-scatter.16.cloned.1.call-update) | async-done | bytes 1048592 | tf_op jit(solution)/shard_map/reduce_scatter | solution.py:310
  1395.8 49.7 %reduce-scatter.12.cloned.1.call-done = bf16[256,512]{1,0:T(8,128)(2,1)} async-done(((bf16[2048,512]{1,0:T(8,128)(2,1)}), bf16[256,512]{1,0:T(8,128)(2,1)}) %reduce-scatter.12.cloned.1.call-update) | async-done | bytes 262160 | tf_op jit(solution)/shard_map/reduce_scatter | solution.py:304
  1447.3 48.6 %reduce-scatter.10.cloned.1.call-done = bf16[256,512]{1,0:T(8,128)(2,1)} async-done(((bf16[2048,512]{1,0:T(8,128)(2,1)}), bf16[256,512]{1,0:T(8,128)(2,1)}) %reduce-scatter.10.cloned.1.call-update) | async-done | bytes 262160 | tf_op jit(solution)/shard_map/reduce_scatter | solution.py:301
  1497.7 48.6 %reduce-scatter.8.cloned.1.call-done = bf16[256,512]{1,0:T(8,128)(2,1)} async-done(((bf16[2048,512]{1,0:T(8,128)(2,1)}), bf16[256,512]{1,0:T(8,128)(2,1)}) %reduce-scatter.8.cloned.1.call-update) | async-done | bytes 262160 | tf_op jit(solution)/shard_map/reduce_scatter | solution.py:298
  1548.2 87.1 %all-gather.30.cloned.1.call-done = bf16[2048,2048]{1,0:T(8,128)(2,1)} async-done(((bf16[512,2048]{1,0:T(8,128)(2,1)}), bf16[2048,2048]{1,0:T(8,128)(2,1)}) %all-gather.30.cloned.1.call-update) | async-done | bytes 8388624 | tf_op jit(solution)/shard_map/all_gather | solution.py:75
  1645.9 16.2 all-reduce.2
  1663.4 44.4 %all-reduce.8.cloned.1.call-done = bf16[512,2048]{1,0:T(8,128)(2,1)} async-done(((bf16[512,2048]{1,0:T(8,128)(2,1)}), bf16[512,2048]{1,0:T(8,128)(2,1)}) %all-reduce.8.cloned.1.call-update) | async-done | bytes 2097168 | tf_op jit(solution)/shard_map/psum | solution.py:71
  (358 shorter events, 387.0 us)
Async XLA Ops:
  7.2 34.5 %all-gather.16.cloned.1.call-start = ((), (), s32[]{:S(2)}) async-start(), calls=%async_computation.8 | async-start | bytes 2359296 | tf_op jit(solution)/shard_map/all_gather | solution.py:150
  7.9 63.9 %all-gather.14.cloned.1.call-start = ((), (), s32[]{:S(2)}) async-start(), calls=%async_computation.7 | async-start | bytes 2359296 | tf_op jit(solution)/shard_map/all_gather | solution.py:149
  8.7 93.3 %all-gather.18.cloned.1.call-start = ((), (), s32[]{:S(2)}) async-start(), calls=%async_computation.9 | async-start | bytes 2359296 | tf_op jit(solution)/shard_map/all_gather | solution.py:148
  9.4 214.8 %all-gather.20.cloned.1.call-start = ((), (), s32[]{:S(2)}) async-start(), calls=%async_computation.10 | async-start | bytes 2359296 | tf_op jit(solution)/shard_map/all_gather | solution.py:151
  10.0 286.3 %all-reduce.6.cloned.1.call-start = ((), (), s32[]{:S(2)}) async-start(), calls=%async_computation.11 | async-start | bytes 4194304 | tf_op jit(solution)/shard_map/psum | solution.py:71
  120.5 33.8 %collective-permute-start.1 = (bf16[512,512]{0,1:T(8,128)(2,1)}, bf16[512,512]{0,1:T(8,128)(2,1)S(1)}, u32[]{:S(2)}, u32[]{:S(2)}) collective-permute-start(bf16[512,512]{0,1:T(8,128)(2,1)} %get-tuple-element.431), channel_id=1, source_target_pairs={{0,4},{4,8},{8,12},{12,0},{1,5},{5,9},{9,13},{13,1},{2,6},{6,10},{... | collective-permute-start | bytes 1572872 | tf_op jit(solution)/shard_map/while/body/eval_jaxpr/ppermute | solution.py:16
  228.5 151.3 %all-gather.24.cloned.1.call-start = ((), (), s32[]{:S(2)}) async-start(), calls=%async_computation.13 | async-start | bytes 9437184 | tf_op jit(solution)/shard_map/all_gather | solution.py:153
  229.0 232.9 %all-gather.22.cloned.1.call-start = ((), (), s32[]{:S(2)}) async-start(), calls=%async_computation.12 | async-start | bytes 9437184 | tf_op jit(solution)/shard_map/all_gather | solution.py:152
  229.8 314.3 %all-gather.26.cloned.1.call-start = ((), (), s32[]{:S(2)}) async-start(), calls=%async_computation.14 | async-start | bytes 9437184 | tf_op jit(solution)/shard_map/all_gather | solution.py:154
  230.5 439.4 %all-gather.28.cloned.1.call-start = ((), (), s32[]{:S(2)}) async-start(), calls=%async_computation.23 | async-start | bytes 10485760 | tf_op jit(solution)/shard_map/all_gather | solution.py:75
  583.8 650.6 %reduce-scatter.14.cloned.1.call-start = ((), (), s32[]{:S(2)}) async-start(), calls=%async_computation.19 | async-start | bytes 2359296 | tf_op jit(solution)/shard_map/reduce_scatter | solution.py:307
  685.8 550.4 %reduce-scatter.20.cloned.1.call-start = ((), (), s32[]{:S(2)}) async-start(), calls=%async_computation.22 | async-start | bytes 9437184 | tf_op jit(solution)/shard_map/reduce_scatter | solution.py:316
  696.0 542.8 %reduce-scatter.18.cloned.1.call-start = ((), (), s32[]{:S(2)}) async-start(), calls=%async_computation.21 | async-start | bytes 9437184 | tf_op jit(solution)/shard_map/reduce_scatter | solution.py:313
  706.6 686.4 %reduce-scatter.16.cloned.1.call-start = ((), (), s32[]{:S(2)}) async-start(), calls=%async_computation.20 | async-start | bytes 9437184 | tf_op jit(solution)/shard_map/reduce_scatter | solution.py:310
  716.7 728.8 %reduce-scatter.12.cloned.1.call-start = ((), (), s32[]{:S(2)}) async-start(), calls=%async_computation.18 | async-start | bytes 2359296 | tf_op jit(solution)/shard_map/reduce_scatter | solution.py:304
  740.8 92.7 %collective-permute-start.9 = (bf16[512,512]{0,1:T(8,128)(2,1)}, bf16[512,512]{0,1:T(8,128)(2,1)}, u32[]{:S(2)}, u32[]{:S(2)}) collective-permute-start(bf16[512,512]{0,1:T(8,128)(2,1)} %get-tuple-element.475), channel_id=1, source_target_pairs={{0,4},{4,8},{8,12},{12,0},{1,5},{5,9},{9,13},{13,1},{2,6},{6,10},{... | collective-permute-start | bytes 1572872 | tf_op jit(solution)/shard_map/while/body/eval_jaxpr/ppermute | solution.py:16
  741.3 97.2 %collective-permute-start.8 = (bf16[512,512]{0,1:T(8,128)(2,1)}, bf16[512,512]{0,1:T(8,128)(2,1)}, u32[]{:S(2)}, u32[]{:S(2)}) collective-permute-start(bf16[512,512]{0,1:T(8,128)(2,1)} %get-tuple-element.474), channel_id=1, source_target_pairs={{0,4},{4,8},{8,12},{12,0},{1,5},{5,9},{9,13},{13,1},{2,6},{6,10},{... | collective-permute-start | bytes 1572872 | tf_op jit(solution)/shard_map/while/body/eval_jaxpr/ppermute | solution.py:16
  760.1 66.2 %collective-permute-start.5 = (bf16[512,512]{0,1:T(8,128)(2,1)}, bf16[512,512]{0,1:T(8,128)(2,1)S(1)}, u32[]{:S(2)}, u32[]{:S(2)}) collective-permute-start(bf16[512,512]{0,1:T(8,128)(2,1)} %get-tuple-element.470), channel_id=1, source_target_pairs={{0,4},{4,8},{8,12},{12,0},{1,5},{5,9},{9,13},{13,1},{2,6},{6,10},{... | collective-permute-start | bytes 1572872 | tf_op jit(solution)/shard_map/while/body/eval_jaxpr/ppermute | solution.py:16
  840.9 60.4 %collective-permute-start.4 = (bf16[512,512]{0,1:T(8,128)(2,1)}, bf16[512,512]{0,1:T(8,128)(2,1)S(1)}, u32[]{:S(2)}, u32[]{:S(2)}) collective-permute-start(bf16[512,512]{0,1:T(8,128)(2,1)} %get-tuple-element.469), channel_id=1, source_target_pairs={{0,4},{4,8},{8,12},{12,0},{1,5},{5,9},{9,13},{13,1},{2,6},{6,10},{... | collective-permute-start | bytes 1572872 | tf_op jit(solution)/shard_map/while/body/eval_jaxpr/ppermute | solution.py:16
  873.1 95.6 %collective-permute-start.9 = (bf16[512,512]{0,1:T(8,128)(2,1)}, bf16[512,512]{0,1:T(8,128)(2,1)}, u32[]{:S(2)}, u32[]{:S(2)}) collective-permute-start(bf16[512,512]{0,1:T(8,128)(2,1)} %get-tuple-element.475), channel_id=1, source_target_pairs={{0,4},{4,8},{8,12},{12,0},{1,5},{5,9},{9,13},{13,1},{2,6},{6,10},{... | collective-permute-start | bytes 1572872 | tf_op jit(solution)/shard_map/while/body/eval_jaxpr/ppermute | solution.py:16
  873.1 100.6 %collective-permute-start.8 = (bf16[512,512]{0,1:T(8,128)(2,1)}, bf16[512,512]{0,1:T(8,128)(2,1)}, u32[]{:S(2)}, u32[]{:S(2)}) collective-permute-start(bf16[512,512]{0,1:T(8,128)(2,1)} %get-tuple-element.474), channel_id=1, source_target_pairs={{0,4},{4,8},{8,12},{12,0},{1,5},{5,9},{9,13},{13,1},{2,6},{6,10},{... | collective-permute-start | bytes 1572872 | tf_op jit(solution)/shard_map/while/body/eval_jaxpr/ppermute | solution.py:16
  896.3 65.2 %collective-permute-start.5 = (bf16[512,512]{0,1:T(8,128)(2,1)}, bf16[512,512]{0,1:T(8,128)(2,1)S(1)}, u32[]{:S(2)}, u32[]{:S(2)}) collective-permute-start(bf16[512,512]{0,1:T(8,128)(2,1)} %get-tuple-element.470), channel_id=1, source_target_pairs={{0,4},{4,8},{8,12},{12,0},{1,5},{5,9},{9,13},{13,1},{2,6},{6,10},{... | collective-permute-start | bytes 1572872 | tf_op jit(solution)/shard_map/while/body/eval_jaxpr/ppermute | solution.py:16
  976.1 57.2 %collective-permute-start.4 = (bf16[512,512]{0,1:T(8,128)(2,1)}, bf16[512,512]{0,1:T(8,128)(2,1)S(1)}, u32[]{:S(2)}, u32[]{:S(2)}) collective-permute-start(bf16[512,512]{0,1:T(8,128)(2,1)} %get-tuple-element.469), channel_id=1, source_target_pairs={{0,4},{4,8},{8,12},{12,0},{1,5},{5,9},{9,13},{13,1},{2,6},{6,10},{... | collective-permute-start | bytes 1572872 | tf_op jit(solution)/shard_map/while/body/eval_jaxpr/ppermute | solution.py:16
  1002.6 97.0 %collective-permute-start.9 = (bf16[512,512]{0,1:T(8,128)(2,1)}, bf16[512,512]{0,1:T(8,128)(2,1)}, u32[]{:S(2)}, u32[]{:S(2)}) collective-permute-start(bf16[512,512]{0,1:T(8,128)(2,1)} %get-tuple-element.475), channel_id=1, source_target_pairs={{0,4},{4,8},{8,12},{12,0},{1,5},{5,9},{9,13},{13,1},{2,6},{6,10},{... | collective-permute-start | bytes 1572872 | tf_op jit(solution)/shard_map/while/body/eval_jaxpr/ppermute | solution.py:16
  1002.6 102.0 %collective-permute-start.8 = (bf16[512,512]{0,1:T(8,128)(2,1)}, bf16[512,512]{0,1:T(8,128)(2,1)}, u32[]{:S(2)}, u32[]{:S(2)}) collective-permute-start(bf16[512,512]{0,1:T(8,128)(2,1)} %get-tuple-element.474), channel_id=1, source_target_pairs={{0,4},{4,8},{8,12},{12,0},{1,5},{5,9},{9,13},{13,1},{2,6},{6,10},{... | collective-permute-start | bytes 1572872 | tf_op jit(solution)/shard_map/while/body/eval_jaxpr/ppermute | solution.py:16
  1025.7 66.6 %collective-permute-start.5 = (bf16[512,512]{0,1:T(8,128)(2,1)}, bf16[512,512]{0,1:T(8,128)(2,1)S(1)}, u32[]{:S(2)}, u32[]{:S(2)}) collective-permute-start(bf16[512,512]{0,1:T(8,128)(2,1)} %get-tuple-element.470), channel_id=1, source_target_pairs={{0,4},{4,8},{8,12},{12,0},{1,5},{5,9},{9,13},{13,1},{2,6},{6,10},{... | collective-permute-start | bytes 1572872 | tf_op jit(solution)/shard_map/while/body/eval_jaxpr/ppermute | solution.py:16
  1107.0 56.0 %collective-permute-start.11 = (bf16[512,512]{0,1:T(8,128)(2,1)}, bf16[512,512]{0,1:T(8,128)(2,1)S(1)}, u32[]{:S(2)}, u32[]{:S(2)}) collective-permute-start(bf16[512,512]{0,1:T(8,128)(2,1)} %get-tuple-element.149), channel_id=1, source_target_pairs={{0,4},{4,8},{8,12},{12,0},{1,5},{5,9},{9,13},{13,1},{2,6},{6,10},{... | collective-permute-start | bytes 1572872 | tf_op jit(solution)/shard_map/ppermute | solution.py:16
  1166.6 329.4 %reduce-scatter.10.cloned.1.call-start = ((), (), s32[]{:S(2)}) async-start(), calls=%async_computation.17 | async-start | bytes 2359296 | tf_op jit(solution)/shard_map/reduce_scatter | solution.py:301
  1166.6 41.2 %collective-permute-start.10 = (bf16[512,512]{0,1:T(8,128)(2,1)S(1)}, bf16[512,512]{0,1:T(8,128)(2,1)S(1)}, u32[]{:S(2)}, u32[]{:S(2)}) collective-permute-start(bf16[512,512]{0,1:T(8,128)(2,1)S(1)} %copy-done.30), channel_id=1, source_target_pairs={{0,4},{4,8},{8,12},{12,0},{1,5},{5,9},{9,13},{13,1},{2,6},{6,10},{... | collective-permute-start | bytes 1572872 | tf_op jit(solution)/shard_map/ppermute | solution.py:16
  1212.4 334.0 %reduce-scatter.8.cloned.1.call-start = ((), (), s32[]{:S(2)}) async-start(), calls=%async_computation.16 | async-start | bytes 2359296 | tf_op jit(solution)/shard_map/reduce_scatter | solution.py:298
  1215.3 420.0 %all-gather.30.cloned.1.call-start = ((), (), s32[]{:S(2)}) async-start(), calls=%async_computation.24 | async-start | bytes 10485760 | tf_op jit(solution)/shard_map/all_gather | solution.py:75
  1222.8 484.9 %all-reduce.8.cloned.1.call-start = ((), (), s32[]{:S(2)}) async-start(), calls=%async_computation.15 | async-start | bytes 4194304 | tf_op jit(solution)/shard_map/psum | solution.py:71
  (78 other events, 2425.5 us)
Sparse Core Ops, SparseCore 0:
  9.6 32.0 all-gather.15
  43.2 28.5 all-gather.13
  73.4 28.5 all-gather.17
  103.4 36.2 all-gather.19
  228.6 67.6 all-reduce.5
  297.7 82.0 all-gather.23
  381.4 80.5 all-gather.21
  463.5 80.5 all-gather.25
  584.0 85.9 all-gather.27
  685.9 49.0 reduce-scatter.13
  737.3 251.9 reduce-scatter.19
  991.5 232.7 reduce-scatter.17
  1226.6 166.3 reduce-scatter.15
  1395.1 50.2 reduce-scatter.11
  1447.6 48.2 reduce-scatter.9
  1498.1 48.2 reduce-scatter.7
  1548.6 86.6 all-gather.29
  1638.3 69.4 all-reduce.7
